TPU v7x, 256 devices: a whole 4x4x8 slice. The times are simulated.
256 devices in a mesh: dp: 16 (over y, x_lo, core), ctx: 8 (over z), tp: 2 (over x_hi).
Axes of the slice: x: 4 (x_hi: 2, x_lo: 2; x = x_hi * 2 + x_lo), y: 4, z: 8, core: 2. Of those that a mesh axis runs over, the one named last changes fastest.
Arguments:
- tokens: bfloat16 [16, 2048, 8192], P('dp', 'ctx', 'tp'), may hold values from -6 to 6
- queries: bfloat16 [16, 2048, 8192], P('dp', 'ctx', 'tp'), may hold values from -180 to 180
- k_weight: bfloat16 [8192, 512], P('dp', 'tp'), may hold values from -0.0625 to 0.0625
- v_weight: bfloat16 [8192, 512], P('dp', 'tp'), may hold values from -0.0625 to 0.0625
- doc_blocks: int32 [16, 16], P('dp', 'ctx'), may hold values from 0 to 3, never falling along the last dimension, each value on 1 to 8 neighbouring positions
Outputs:
- context: bfloat16 [16, 2048, 8192], P('dp', 'ctx', 'tp')
Inputs may be any that keep to these rules, and one draw needn't show every extreme that they name: `doc_blocks`: along each sequence the document numbers never fall; each document covers 1 to 8 whole blocks, one exactly 8.
All inputs are finite; a program needn't handle non-finite values.
Results may differ from a plain program's by a relative error of at most 0.012.
The roundings to bfloat16 on the way count: a program that leaves them out, or rounds other values in their place, can miss the bound.
Values may be sent and summed in bfloat16 or wider, within the bound.
No kernel may reach another device: no remote copies, remote signals or barrier semaphores. Data moves between devices by JAX's collectives and lax.ppermute only.
A program may use at most 192 MiB of HBM per device.

v0:
```python
import math
import jax
import jax.numpy as jnp
from jax import lax
from jax.sharding import PartitionSpec as P

HD = 128
BLOCK = 128
ROPE_BASE = 500000.0
YARN_FACTOR = 16.0
PRETRAIN_CONTEXT = 8192.0
BETA_FAST = 32.0
BETA_SLOW = 1.0
ATTN_FACTOR = (1.0 + 0.1 * math.log(16.0)) ** 2
MASKED_SCORE = -1e30


def yarn_tables(positions):
    counter = jnp.arange(HD // 2, dtype=jnp.float32)
    base_freq = ROPE_BASE ** (-2.0 * counter / HD)
    wave_ratio = PRETRAIN_CONTEXT * base_freq / (2.0 * math.pi)
    ramp_value = jnp.clip((wave_ratio - BETA_SLOW) / (BETA_FAST - BETA_SLOW), 0.0, 1.0)
    frequency = ramp_value * base_freq + (1.0 - ramp_value) * base_freq / YARN_FACTOR
    angles = positions.astype(jnp.float32)[:, None] * frequency[None, :]
    cosine = jnp.cos(angles)
    sine_table = jnp.sin(angles)
    return (
        jnp.concatenate([cosine, cosine], axis=-1),
        jnp.concatenate([sine_table, sine_table], axis=-1),
    )


def rotate(vectors, cosine, sine_table):
    half_width = vectors.shape[-1] // 2
    lower_half = vectors[..., :half_width]
    upper_half = vectors[..., half_width:]
    turned = jnp.concatenate([-upper_half, lower_half], axis=-1)
    return vectors * cosine[:, None, :] + turned * sine_table[:, None, :]


def collect_features(local_tokens):
    return lax.all_gather(local_tokens, "tp", axis=1, tiled=True)


def body(tokens, queries, k_weight, v_weight, doc_blocks):
    local_tokens = tokens[0]
    row_count = local_tokens.shape[0]
    ctx_rank = lax.axis_index("ctx")
    all_docs = lax.all_gather(doc_blocks[0], "ctx", axis=0, tiled=True)
    kv_width = k_weight.shape[1]
    kv_heads = kv_width // HD
    whole = collect_features(local_tokens)
    pieces = (
        lax.all_gather(k_weight, "dp", axis=0, tiled=True),
        lax.all_gather(v_weight, "dp", axis=0, tiled=True),
    )
    height = pieces[0].shape[0]
    key_proj = jnp.dot(whole, pieces[0], preferred_element_type=jnp.float32)
    value_proj = jnp.dot(whole, pieces[1], preferred_element_type=jnp.float32)
    positions = ctx_rank * row_count + jnp.arange(row_count, dtype=jnp.int32)
    cosine, sine_table = yarn_tables(positions)
    key_rows = (
        rotate(key_proj.reshape(row_count, kv_heads, HD), cosine, sine_table)
        .reshape(row_count, kv_width)
        .astype(jnp.bfloat16)
    )
    value_rows = value_proj.astype(jnp.bfloat16)
    local_queries = queries[0]
    query_heads = local_queries.shape[1] // HD
    group_size = query_heads // kv_heads
    query_rot = (
        (
            rotate(
                local_queries.astype(jnp.float32).reshape(row_count, query_heads, HD),
                cosine,
                sine_table,
            )
            * (ATTN_FACTOR / math.sqrt(HD))
        )
        .reshape(row_count, query_heads * HD)
        .astype(jnp.bfloat16)
    )
    token_docs = jnp.repeat(all_docs, BLOCK)
    query_total = query_rot.shape[0]
    query_docs = token_docs[positions]
    grouped = query_rot.reshape(query_total, kv_heads, group_size, HD)
    start_max = jnp.full((kv_heads, group_size, query_total), MASKED_SCORE, jnp.float32)
    start_sum = jnp.zeros((kv_heads, group_size, query_total), jnp.float32)
    start_acc = jnp.zeros((kv_heads, group_size, query_total, HD), jnp.float32)
    key_piece = lax.all_gather(key_rows, "ctx", axis=0, tiled=True)
    value_piece = lax.all_gather(value_rows, "ctx", axis=0, tiled=True)
    height = key_piece.shape[0]
    key_pos = jnp.arange(height, dtype=jnp.int32)
    visible = (key_pos[None, :] <= positions[:, None]) & (
        token_docs[None, :] == query_docs[:, None]
    )

    def update(state):
        running_max, running_sum, running_acc = state
        scores = jnp.einsum(
            "qkgd,nkd->kgqn",
            grouped,
            key_piece.reshape(height, kv_heads, HD),
            preferred_element_type=jnp.float32,
        )
        scores = jnp.where(visible, scores, MASKED_SCORE)
        new_max = jnp.maximum(running_max, jnp.max(scores, axis=-1))
        weights = jnp.where(visible, jnp.exp(scores - new_max[..., None]), 0.0)
        new_sum = jnp.sum(weights, axis=-1)
        new_acc = jnp.einsum(
            "kgqn,nkd->kgqd",
            weights.astype(jnp.bfloat16),
            value_piece.reshape(height, kv_heads, HD),
            preferred_element_type=jnp.float32,
        )
        return (new_max, new_sum, new_acc)

    def unchanged(state):
        return state

    final_max, final_sum, final_acc = lax.cond(
        jnp.any(visible), update, unchanged, (start_max, start_sum, start_acc)
    )
    attended = final_acc / final_sum[..., None]
    context = (
        attended.transpose(2, 0, 1, 3).reshape(query_total, query_heads * HD).astype(jnp.bfloat16)
    )
    return context[None]


def solution(mesh):
    placed = (
        P("dp", "ctx", "tp"),
        P("dp", "ctx", "tp"),
        P("dp", "tp"),
        P("dp", "tp"),
        P("dp", "ctx"),
    )
    return jax.shard_map(
        body, mesh=mesh, in_specs=placed, out_specs=P("dp", "ctx", "tp"), check_vma=False
    )
```

profile of v0, /device:TPU:2, one launch (start us, length us, event | category | flops | bytes accessed | tf_op | source)
XLA Modules:
  0.0 327.5 jit_solution(8934308022742542548)
XLA Ops:
  6.5 0.7 all-gather.16.cloned.1.call-update
  9.2 65.3 %all-gather.16.cloned.1.call-done = bf16[1,256,8192]{2,1,0:T(8,128)(2,1)} async-done(((bf16[1,256,4096]{2,1,0:T(8,128)(2,1)}), bf16[1,256,8192]{2,1,0:T(8,128)(2,1)}) %all-gather.16.cloned.1.call-update) | async-done | bytes 4194320 | tf_op jit(solution)/shard_map/all_gather | solution.py:42
  74.5 41.7 %all-gather.8.cloned.1.call-done = bf16[8192,256]{1,0:T(8,128)(2,1)} async-done(((bf16[512,256]{1,0:T(8,128)(2,1)}), bf16[8192,256]{1,0:T(8,128)(2,1)}) %all-gather.8.cloned.1.call-update) | async-done | bytes 4194320 | tf_op jit(solution)/shard_map/all_gather | solution.py:54
  116.2 5.2 %fusion.11 = f32[256,256]{0,1:T(8,128)S(1)} fusion(bf16[8192,256]{1,0:T(8,128)(2,1)} %all-gather.8.cloned.1.call-done, bf16[1,256,8192]{2,1,0:T(8,128)(2,1)} %all-gather.16.cloned.1.call-done), kind=kOutput, calls=%fused_computation.15 | convolution fusion | flops 1073741824 | bytes 8650752 | tf_op jit(solution)/shard_map/dot_general | solution.py:58
  123.6 34.4 %all-gather.12.cloned.1.call-done = bf16[8192,256]{1,0:T(8,128)(2,1)} async-done(((bf16[512,256]{1,0:T(8,128)(2,1)}), bf16[8192,256]{1,0:T(8,128)(2,1)}) %all-gather.12.cloned.1.call-update) | async-done | bytes 4194320 | tf_op jit(solution)/shard_map/all_gather | solution.py:55
  157.9 5.4 %fusion.15 = bf16[256,256]{1,0:T(8,128)(2,1)} fusion(bf16[8192,256]{1,0:T(8,128)(2,1)} %all-gather.12.cloned.1.call-done, bf16[1,256,8192]{2,1,0:T(8,128)(2,1)} %all-gather.16.cloned.1.call-done), kind=kOutput, calls=%fused_computation.23 | convolution fusion | flops 1073807360 | bytes 8519680 | tf_op jit(solution)/shard_map/dot_general | solution.py:59
  163.3 3.3 %copy.18 = bf16[1,256,4096]{1,2,0:T(8,128)(2,1)S(1)} copy(bf16[1,256,4096]{2,1,0:T(8,128)(2,1)} %param.8) | data formatting | bytes 4194304 | tf_op args[1]
  166.6 2.3 convert_element_type.65
  168.9 14.0 %all-reduce = s32[16]{0:T(128)S(1)} all-reduce(s32[16]{0:T(128)S(1)} %bitcast_dynamic-update-slice_fusion), channel_id=2, replica_groups=mesh['dp'=16,'ctx'=8,'tp'=2] {'ctx'}, use_global_device_ids=true, to_apply=%add | all-reduce | flops 16 | bytes 128
  183.0 1.7 gather_fusion
  184.8 1.3 fusion.14
  186.6 2.5 slice_negate_fusion
  189.6 1.8 copy-done
  191.3 1.1 multiply_convert_fusion
  192.4 6.9 %all-gather.10.cloned.1.call-done = bf16[2048,256]{0,1:T(8,128)(2,1)} async-done(((bf16[256,256]{0,1:T(8,128)(2,1)}), bf16[2048,256]{0,1:T(8,128)(2,1)}) %all-gather.10.cloned.1.call-update) | async-done | bytes 1048592 | tf_op jit(solution)/shard_map/all_gather | solution.py:90
  199.3 39.1 %all-gather.14.cloned.1.call-done = bf16[2048,256]{1,0:T(8,128)(2,1)} async-done(((bf16[256,256]{1,0:T(8,128)(2,1)}), bf16[2048,256]{1,0:T(8,128)(2,1)}) %all-gather.14.cloned.1.call-update) | async-done | bytes 1048592 | tf_op jit(solution)/shard_map/all_gather | solution.py:91
  238.4 76.0 %conditional.1 = (f32[2,16,256]{2,1,0:T(8,128)S(1)}, f32[2,16,256,128]{3,2,1,0:T(8,128)}) conditional(s32[]{:T(128)} %convert_element_type.53, () %tuple.13, (pred[256,2048]{0,1:T(8,128)(4,1)S(1)}, bf16[2048,256]{0,1:T(8,128)(2,1)}, bf16[256,2,16,128]{0,3,2,1:T(8,128)(2,1)S(1)}, bf16[2048,256]{1,0:T(8,128)(2,1)}) %tuple.14), branch_computations={%region_1.2_spmd, %region_2.5_spmd} | conditional | flops 8757698560 | bytes 213581840 | solution.py:121
  238.4 24.4 %fusion = (f32[2,16,256]{2,1,0:T(8,128)S(1)}, f32[2,2048,256,16]{2,1,3,0:T(8,128)}) fusion(pred[256,2048]{0,1:T(8,128)(4,1)S(1)} %get-tuple-element.13, bf16[2048,2,128,1]{0,2,3,1:T(8,128)(2,1)} %bitcast.55, bf16[256,2,16,128]{0,3,2,1:T(8,128)(2,1)S(1)} %get-tuple-element.27), kind=kOutput, calls=%fused_computation.3 | convolution fusion | flops 4328513536 | bytes 70811648 | tf_op jit(solution)/shard_map/cond/branch_1_fun/qkgd,nkd->kgqn/dot_general | solution.py:100
  262.8 1.3 reshape.84
  264.1 28.7 %fusion.3 = f32[2,16,256,128]{3,2,1,0:T(8,128)} fusion(f32[2,2048,256,16]{2,1,3,0:T(8,128)} %get-tuple-element.30, f32[2,16,256]{2,1,0:T(8,128)S(1)} %broadcast_maximum_fusion, pred[256,2048]{0,1:T(8,128)(4,1)S(1)} %get-tuple-element.13, bf16[2048,2,128,1]{2,1,0,3:T(2,128)(2,1)S(1)} %bitcast.54), kind=kOutput, calls=%fused_computation.6 | convolution fusion | flops 4362076160 | bytes 72908800 | tf_op jit(solution)/shard_map/cond/branch_1_fun/kgqn,nkd->kgqd/dot_general | solution.py:110
  292.9 21.6 %fusion.2 = f32[2,16,256]{2,1,0:T(8,128)S(1)} fusion(f32[2,2048,256,16]{2,1,3,0:T(8,128)} %get-tuple-element.30, f32[2,16,256]{2,1,0:T(8,128)S(1)} %broadcast_maximum_fusion, pred[256,2048]{0,1:T(8,128)(4,1)S(1)} %get-tuple-element.13), kind=kLoop, calls=%fused_computation.5 | loop fusion | flops 67100672 | bytes 67698688 | tf_op jit(solution)/shard_map/cond/branch_1_fun/reduce_sum | solution.py:109
  314.5 2.9 fusion.13
  317.3 1.4 copy.21
  318.7 2.3 convert_element_type.64
  (30 shorter events, 3.9 us)
Async XLA Ops:
  6.5 68.0 %all-gather.16.cloned.1.call-start = ((), (), s32[]{:S(2)}) async-start(), calls=%async_computation.4 | async-start | bytes 6291456 | tf_op jit(solution)/shard_map/all_gather | solution.py:42
  7.3 109.0 %all-gather.8.cloned.1.call-start = ((), (), s32[]{:S(2)}) async-start(), calls=%async_computation | async-start | bytes 4456448 | tf_op jit(solution)/shard_map/all_gather | solution.py:54
  8.0 149.9 %all-gather.12.cloned.1.call-start = ((), (), s32[]{:S(2)}) async-start(), calls=%async_computation.2 | async-start | bytes 4456448 | tf_op jit(solution)/shard_map/all_gather | solution.py:55
  8.7 190.6 %all-gather.10.cloned.1.call-start = ((), (), s32[]{:S(2)}) async-start(), calls=%async_computation.1 | async-start | bytes 1179648 | tf_op jit(solution)/shard_map/all_gather | solution.py:90
  9.2 113.1 %copy-start.2 = (u32[256]{0:T(256)S(1)}, u32[256]{0:T(256)}, u32[]{:S(2)}) copy-start(u32[256]{0:T(256)} %constant.56) | copy-start | bytes 3076
  9.2 114.3 %copy-start.1 = (s32[1,2]{1,0:T(1,128)S(1)}, s32[1,2]{1,0:T(1,128)}, u32[]{:S(2)}) copy-start(s32[1,2]{1,0:T(1,128)} %param.11) | copy-start | bytes 28
  122.2 116.2 %all-gather.14.cloned.1.call-start = ((), (), s32[]{:S(2)}) async-start(), calls=%async_computation.3 | async-start | bytes 1179648 | tf_op jit(solution)/shard_map/all_gather | solution.py:91
  189.1 2.2 copy-start
Sparse Core Ops, SparseCore 0:
  9.1 65.3 all-gather.15
  76.4 39.8 all-gather.7
  118.1 39.7 all-gather.11
  159.5 39.7 all-gather.9
  200.9 37.4 all-gather.13
where the time goes:
time: 328 us
  waiting for transfers between devices  190 us (58%)
  matrix products  63.7 us (19%)
  other arithmetic  33.1 us (10%)
  between operations  14.4 us (4%)
  blocking collectives  14 us (4%)
  local copies, waits for them, and re-layouts  12.5 us (4%)
    all_gather x1, waiting for transfers between devices, collect_features(): return lax.all_gather(local_tokens, 'tp', axis=1, tiled=True)  65.3 us
    all_gather x1, waiting for transfers between devices, body(): lax.all_gather(k_weight, 'dp', axis=0, tiled=True)  41.7 us
    all_gather x1, waiting for transfers between devices, body(): value_piece = lax.all_gather(value_rows, 'ctx', axis=0, tiled=True)  39.1 us
    all_gather x1, waiting for transfers between devices, body(): lax.all_gather(v_weight, 'dp', axis=0, tiled=True)  34.4 us
    dot_general x1, matrix products, update(): jnp.einsum('kgqn,nkd->kgqd', weights.astype(jnp.bfloat16), value_piece.re...  28.7 us
    dot_general x1, matrix products, update(): jnp.einsum('qkgd,nkd->kgqn', grouped, key_piece.reshape(height, kv_heads,...  24.4 us
    reduce_sum x1, other arithmetic, update(): new_sum = jnp.sum(weights, axis=-1)  21.6 us
    unnamed x1, blocking collectives  14 us
  transfers between devices with their start and end apart: 5, of which 5 were waited for; matrix products, arithmetic and copies ran while one was open for 8% of the time, Pallas kernels for 0%

commit v1 on v0

--- a/solution.py
+++ b/solution.py
@@ -87,7 +87,9 @@
     start_max = jnp.full((kv_heads, group_size, query_total), MASKED_SCORE, jnp.float32)
     start_sum = jnp.zeros((kv_heads, group_size, query_total), jnp.float32)
     start_acc = jnp.zeros((kv_heads, group_size, query_total, HD), jnp.float32)
-    key_piece = lax.all_gather(key_rows, "ctx", axis=0, tiled=True)
+    key_piece = jnp.concatenate(
+        lax.all_to_all(jnp.stack([key_rows] * lax.axis_size("ctx")), "ctx", 0, 0), axis=0
+    )
     value_piece = lax.all_gather(value_rows, "ctx", axis=0, tiled=True)
     height = key_piece.shape[0]
     key_pos = jnp.arange(height, dtype=jnp.int32)

time: 328 us -> 294 us (0.90)
  waiting for transfers between devices: 190 us -> 145 us
  starting transfers between devices: 0.16 us -> 7.13 us
  local copies, waits for them, and re-layouts: 12.5 us -> 17.1 us
    all_gather x1, waiting for transfers between devices: 39.1 us -> 9.93 us  [body(): value_piece = lax.all_gather(value_rows, 'ctx', axis=0, tiled=True)]
    all_to_all x0 -> x1, starting transfers between devices: none -> 7.01 us  [body(): lax.all_to_all(jnp.stack([key_rows] * lax.axis_size('ctx')), 'ctx', 0, 0)]
    all_gather x1 -> x0, waiting for transfers between devices: 6.88 us -> none  [body(): key_piece = lax.all_gather(key_rows, 'ctx', axis=0, tiled=True)]
    all_gather x1, waiting for transfers between devices: 34.4 us -> 28.2 us  [body(): lax.all_gather(v_weight, 'dp', axis=0, tiled=True)]
    unnamed x10 -> x6, local copies, waits for them, and re-layouts: 5.72 us -> 7.02 us
  transfers between devices with their start and end apart: 5 -> 5, of which waited for: 5 -> 4; matrix products, arithmetic and copies ran while one was open for 8% -> 9% of each run, Pallas kernels for 0% -> 0%
where the time goes in v1:
time: 294 us
  waiting for transfers between devices  145 us (49%)
  matrix products  63.8 us (22%)
  other arithmetic  32.6 us (11%)
  local copies, waits for them, and re-layouts  17.1 us (6%)
  between operations  14.5 us (5%)
  blocking collectives  13.9 us (5%)
  starting transfers between devices  7.13 us (2%)
    all_gather x1, waiting for transfers between devices, collect_features(): return lax.all_gather(local_tokens, 'tp', axis=1, tiled=True)  62.7 us
    all_gather x1, waiting for transfers between devices, body(): lax.all_gather(k_weight, 'dp', axis=0, tiled=True)  41.7 us
    dot_general x1, matrix products, update(): jnp.einsum('kgqn,nkd->kgqd', weights.astype(jnp.bfloat16), value_piece.re...  28.7 us
    all_gather x1, waiting for transfers between devices, body(): lax.all_gather(v_weight, 'dp', axis=0, tiled=True)  28.2 us
    dot_general x1, matrix products, update(): jnp.einsum('qkgd,nkd->kgqn', grouped, key_piece.reshape(height, kv_heads,...  24.5 us
    reduce_sum x1, other arithmetic, update(): new_sum = jnp.sum(weights, axis=-1)  21.6 us
    unnamed x1, blocking collectives  13.9 us
    all_gather x1, waiting for transfers between devices, body(): value_piece = lax.all_gather(value_rows, 'ctx', axis=0, tiled=True)  9.93 us
  transfers between devices with their start and end apart: 5, of which 4 were waited for; matrix products, arithmetic and copies ran while one was open for 9% of the time, Pallas kernels for 0%

profile of v1, /device:TPU:2, one launch (start us, length us, event | category | flops | bytes accessed | tf_op | source)
XLA Modules:
  0.0 293.7 jit_solution(6552430667657631299)
XLA Ops:
  8.7 1.3 dynamic-slice
  11.8 62.7 %all-gather.13.cloned.1.call-done = bf16[1,256,8192]{2,1,0:T(8,128)(2,1)} async-done(((bf16[1,256,4096]{2,1,0:T(8,128)(2,1)}), bf16[1,256,8192]{2,1,0:T(8,128)(2,1)}) %all-gather.13.cloned.1.call-update) | async-done | bytes 4194320 | tf_op jit(solution)/shard_map/all_gather | solution.py:42
  74.5 41.7 %all-gather.7.cloned.1.call-done = bf16[8192,256]{1,0:T(8,128)(2,1)} async-done(((bf16[512,256]{1,0:T(8,128)(2,1)}), bf16[8192,256]{1,0:T(8,128)(2,1)}) %all-gather.7.cloned.1.call-update) | async-done | bytes 4194320 | tf_op jit(solution)/shard_map/all_gather | solution.py:54
  116.2 5.2 %fusion.13 = f32[256,256]{0,1:T(8,128)S(1)} fusion(bf16[8192,256]{1,0:T(8,128)(2,1)} %all-gather.7.cloned.1.call-done, bf16[1,256,8192]{2,1,0:T(8,128)(2,1)} %all-gather.13.cloned.1.call-done), kind=kOutput, calls=%fused_computation.17 | convolution fusion | flops 1073741824 | bytes 8650752 | tf_op jit(solution)/shard_map/dot_general | solution.py:58
  122.7 7.0 %all-to-all-start = ((bf16[8,256,256]{2,1,0:T(8,128)(2,1)}), bf16[8,256,256]{2,1,0:T(8,128)(2,1)}, u32[]{:S(2)}, u32[]{:S(2)}) async-start(bf16[8,256,256]{2,1,0:T(8,128)(2,1)} %stack.2), calls=%async_computation | async-start | bytes 2097152 | tf_op jit(solution)/shard_map/all_to_all | solution.py:91
  129.8 28.2 %all-gather.9.cloned.1.call-done = bf16[8192,256]{1,0:T(8,128)(2,1)} async-done(((bf16[512,256]{1,0:T(8,128)(2,1)}), bf16[8192,256]{1,0:T(8,128)(2,1)}) %all-gather.9.cloned.1.call-update) | async-done | bytes 4194320 | tf_op jit(solution)/shard_map/all_gather | solution.py:55
  157.9 5.4 %fusion.17 = bf16[256,256]{1,0:T(8,128)(2,1)} fusion(bf16[8192,256]{1,0:T(8,128)(2,1)} %all-gather.9.cloned.1.call-done, bf16[1,256,8192]{2,1,0:T(8,128)(2,1)} %all-gather.13.cloned.1.call-done), kind=kOutput, calls=%fused_computation.25 | convolution fusion | flops 1073807360 | bytes 8519680 | tf_op jit(solution)/shard_map/dot_general | solution.py:59
  163.4 3.3 %copy.19 = bf16[1,256,4096]{1,2,0:T(8,128)(2,1)S(1)} copy(bf16[1,256,4096]{2,1,0:T(8,128)(2,1)} %param.8) | data formatting | bytes 4194304 | tf_op args[1]
  166.6 2.3 convert_element_type.65
  168.9 13.9 %all-reduce = s32[16]{0:T(128)S(1)} all-reduce(s32[16]{0:T(128)S(1)} %bitcast_dynamic-update-slice_fusion), channel_id=2, replica_groups=mesh['dp'=16,'ctx'=8,'tp'=2] {'ctx'}, use_global_device_ids=true, to_apply=%add | all-reduce | flops 16 | bytes 128
  182.9 1.7 gather_fusion
  184.7 1.3 fusion.16
  186.6 2.6 slice_negate_fusion
  189.6 1.7 copy-done
  192.4 9.9 %all-gather.11.cloned.1.call-done = bf16[2048,256]{1,0:T(8,128)(2,1)} async-done(((bf16[256,256]{1,0:T(8,128)(2,1)}), bf16[2048,256]{1,0:T(8,128)(2,1)}) %all-gather.11.cloned.1.call-update) | async-done | bytes 1048592 | tf_op jit(solution)/shard_map/all_gather | solution.py:93
  202.3 78.3 %conditional.1 = (f32[2,16,256]{2,1,0:T(8,128)S(1)}, f32[2,16,256,128]{3,2,1,0:T(8,128)}) conditional(s32[]{:T(128)} %convert_element_type.53, () %tuple.13, (pred[256,2048]{0,1:T(8,128)(4,1)S(1)}, bf16[8,256,256]{2,1,0:T(8,128)(2,1)}, bf16[256,2,16,128]{0,3,2,1:T(8,128)(2,1)S(1)}, bf16[2048,256]{1,0:T(8,128)(2,1)}) %tuple.14), branch_computations={%region_1.2_spmd, %region_2.5_spmd} | conditional | flops 8757698560 | bytes 215678992 | solution.py:123
  202.3 2.1 reshape_reshape.2
  204.4 24.5 %fusion = (f32[2,16,256]{2,1,0:T(8,128)S(1)}, f32[2,2048,256,16]{2,1,3,0:T(8,128)}) fusion(pred[256,2048]{0,1:T(8,128)(4,1)S(1)} %get-tuple-element.13, bf16[256,2,16,128]{0,3,2,1:T(8,128)(2,1)S(1)} %get-tuple-element.23, bf16[2048,2,128,1]{2,1,0,3:T(2,128)(2,1)} %bitcast.48), kind=kOutput, calls=%fused_computation.3 | convolution fusion | flops 4328513536 | bytes 70811648 | tf_op jit(solution)/shard_map/cond/branch_1_fun/qkgd,nkd->kgqn/dot_general | solution.py:102
  229.0 1.3 reshape.83
  230.3 28.7 %fusion.3 = f32[2,16,256,128]{3,2,1,0:T(8,128)} fusion(f32[2,2048,256,16]{2,1,3,0:T(8,128)} %get-tuple-element.26, f32[2,16,256]{2,1,0:T(8,128)S(1)} %broadcast_maximum_fusion, pred[256,2048]{0,1:T(8,128)(4,1)S(1)} %get-tuple-element.13, bf16[2048,2,128,1]{2,1,0,3:T(2,128)(2,1)S(1)} %bitcast.50), kind=kOutput, calls=%fused_computation.6 | convolution fusion | flops 4362076160 | bytes 72908800 | tf_op jit(solution)/shard_map/cond/branch_1_fun/kgqn,nkd->kgqd/dot_general | solution.py:112
  259.1 21.6 %fusion.2 = f32[2,16,256]{2,1,0:T(8,128)S(1)} fusion(f32[2,2048,256,16]{2,1,3,0:T(8,128)} %get-tuple-element.26, f32[2,16,256]{2,1,0:T(8,128)S(1)} %broadcast_maximum_fusion, pred[256,2048]{0,1:T(8,128)(4,1)S(1)} %get-tuple-element.13), kind=kLoop, calls=%fused_computation.5 | loop fusion | flops 67100672 | bytes 67698688 | tf_op jit(solution)/shard_map/cond/branch_1_fun/reduce_sum | solution.py:111
  280.7 2.9 fusion.15
  283.5 1.4 copy.21
  284.9 2.3 convert_element_type.64
  (28 shorter events, 6.2 us)
Async XLA Ops:
  6.5 68.0 %all-gather.13.cloned.1.call-start = ((), (), s32[]{:S(2)}) async-start(), calls=%async_computation.4 | async-start | bytes 6291456 | tf_op jit(solution)/shard_map/all_gather | solution.py:42
  7.3 109.0 %all-gather.7.cloned.1.call-start = ((), (), s32[]{:S(2)}) async-start(), calls=%async_computation.1 | async-start | bytes 4456448 | tf_op jit(solution)/shard_map/all_gather | solution.py:54
  8.0 149.9 %all-gather.9.cloned.1.call-start = ((), (), s32[]{:S(2)}) async-start(), calls=%async_computation.2 | async-start | bytes 4456448 | tf_op jit(solution)/shard_map/all_gather | solution.py:55
  122.7 69.7 %all-to-all-start = ((bf16[8,256,256]{2,1,0:T(8,128)(2,1)}), bf16[8,256,256]{2,1,0:T(8,128)(2,1)}, u32[]{:S(2)}, u32[]{:S(2)}) async-start(bf16[8,256,256]{2,1,0:T(8,128)(2,1)} %stack.2), calls=%async_computation | async-start | bytes 2097152 | tf_op jit(solution)/shard_map/all_to_all | solution.py:91
  129.7 72.6 %all-gather.11.cloned.1.call-start = ((), (), s32[]{:S(2)}) async-start(), calls=%async_computation.3 | async-start | bytes 1179648 | tf_op jit(solution)/shard_map/all_gather | solution.py:93
  189.1 2.2 copy-start
Sparse Core Ops, SparseCore 0:
  9.1 65.3 all-gather.12
  76.4 39.8 all-gather.6
  118.1 39.7 all-gather.8
  163.5 38.8 all-gather.10
